TPU v7x, 512 devices: a whole 4x8x8 slice. The times are simulated.
512 devices in a mesh: tok: 128 (over z, y, core), rep: 4 (over x).
Axes of the slice: x: 4, y: 8, z: 8, core: 2. Of those that a mesh axis runs over, the one named last changes fastest.
Arguments:
- hidden: bfloat16 [12288, 1024], P(('tok', 'rep')), may hold values from -50 to 50
- norm_gain: bfloat16 [1024], replicated, may hold values from 0.5 to 1.5
- head_weight: bfloat16 [32128, 1024], P('tok'), may hold values from -3.75 to 3.75
- targets: int32 [12288], P(('tok', 'rep')), may hold values from 0 to 32127
- lengths: int32 [64], replicated, may hold values from 96 to 288, as said below
- padding_mask: int32 [12288], P(('tok', 'rep')), may hold values from 0 to 1, as said below
- owner_map: int32 [64], replicated, may hold values from 0 to 511, as said below
Outputs:
- logprob: float32 [12288], P(('tok', 'rep'))
- entropy: float32 [12288], P(('tok', 'rep'))
- request_table: float32 [512, 2, 2], P(('tok', 'rep'))
Inputs may be any that keep to these rules, and one draw needn't show every extreme that they name: `lengths`: lengths sum to 12288; the largest is exactly 288. `padding_mask`: the last token of every sequence is live. Each device's block of 24 tokens holds at most 18 live tokens, and the first block exactly 18. `owner_map`: each device owns at most 2 requests, and some device exactly 2.
All inputs are finite; a program needn't handle non-finite values.
Results may differ from a plain program's by a relative error of at most 0.015.
The roundings to bfloat16 on the way count: a program that leaves them out, or rounds other values in their place, can miss the bound.
Values may be sent and summed in bfloat16 or wider, within the bound.
No kernel may reach another device: no remote copies, remote signals or barrier semaphores. Data moves between devices by JAX's collectives and lax.ppermute only.
A program may use at most 64 MiB of HBM per device.

v0:
```python
import jax
import jax.numpy as jnp
import numpy as np
from jax import lax
from jax.sharding import Mesh
from jax.sharding import PartitionSpec as P

SLOTS = 2
EPSILON = 1e-06
NEG_FILL = -1e30
AXES = ("z", "y", "c", "x")
PLANE = ("z", "y")
CHIP = ("c", "x")


def slice_stats(rows, ids, vocab, vocab_ids):
    logits = lax.dot_general(
        rows, vocab, (((rows.ndim - 1,), (1,)), ((), ())), preferred_element_type=jnp.float32
    )
    row_top = jnp.max(logits, axis=-1)
    weights = jnp.exp(logits - row_top[..., None])
    row_total = jnp.sum(weights, axis=-1)
    moment = jnp.sum(weights * logits, axis=-1)
    chosen = jnp.sum(jnp.where(vocab_ids == ids[..., None], logits, 0.0), axis=-1)
    return (row_top, row_total, moment, chosen)


def gather_by_sum(block, axis):
    count = lax.axis_size(axis)
    place = lax.axis_index(axis)
    buffer = jnp.zeros((count,) + block.shape, block.dtype)
    buffer = lax.dynamic_update_slice(buffer, block[None], (place,) + (0,) * block.ndim)
    return lax.psum(buffer, axis)


def shards(hidden, norm_gain, head_weight, targets, lengths, padding_mask, owner_map):
    nz, ny, nc, nx = (lax.axis_size(a) for a in AXES)
    z, y, c, x = (lax.axis_index(a) for a in AXES)
    plane_count = nz * ny
    chip_count = nc * nx
    local_rows, width = hidden.shape
    slice_width = head_weight.shape[0]
    seq_count = lengths.shape[0]
    tok_place = (z * ny + y) * nc + c
    device_place = tok_place * nx + x
    widened = hidden.astype(jnp.float32)
    mean_square = jnp.mean(widened * widened, axis=1)
    normed = (
        widened * lax.rsqrt(mean_square + EPSILON)[:, None] * norm_gain.astype(jnp.float32)[None, :]
    ).astype(jnp.bfloat16)
    state_norm = jnp.sqrt(mean_square)
    live_row = padding_mask == 1
    other_head = lax.ppermute(head_weight, "c", [(i, (i + 1) % nc) for i in range(nc)])
    other_place = (z * ny + y) * nc + (c + nc - 1) % nc
    vocab = jnp.concatenate([head_weight, other_head], axis=0)
    vocab_ids = jnp.concatenate(
        [
            tok_place * slice_width + jnp.arange(slice_width, dtype=jnp.int32),
            other_place * slice_width + jnp.arange(slice_width, dtype=jnp.int32),
        ]
    )
    meta = jnp.zeros((width,), jnp.float32)
    meta = meta.at[0:local_rows].set((targets // 256).astype(jnp.float32))
    meta = meta.at[local_rows : 2 * local_rows].set((targets % 256).astype(jnp.float32))
    meta = meta.at[2 * local_rows : 3 * local_rows].set(live_row.astype(jnp.float32))
    packet = jnp.concatenate([normed, meta.astype(jnp.bfloat16)[None, :]], axis=0)
    gathered = gather_by_sum(gather_by_sum(packet, "y"), "z")
    gathered = gathered.reshape(plane_count, local_rows + 1, width)
    meta_all = gathered[:, local_rows, :].astype(jnp.float32)
    piece_ids = (
        meta_all[:, 0:local_rows] * 256.0 + meta_all[:, local_rows : 2 * local_rows]
    ).astype(jnp.int32)
    piece_live = meta_all[:, 2 * local_rows : 3 * local_rows] > 0.5
    ids_full = jnp.concatenate([piece_ids, jnp.zeros((plane_count, 1), jnp.int32)], axis=1)
    top_p, total_p, moment_p, chosen_p = (
        part[:, :local_rows] for part in slice_stats(gathered, ids_full, vocab, vocab_ids)
    )
    seq_ends = jnp.cumsum(lengths)
    seq_ids = jnp.arange(seq_count, dtype=jnp.int32)
    block_of = (jnp.arange(plane_count, dtype=jnp.int32) * nc + c) * nx + x
    piece_rows = block_of[:, None] * local_rows + jnp.arange(local_rows, dtype=jnp.int32)[None, :]
    piece_seq = jnp.sum(
        (seq_ends[None, None, :] <= piece_rows[:, :, None]).astype(jnp.int32), axis=2
    )
    member = (piece_seq[:, :, None] == seq_ids[None, None, :]) & piece_live[:, :, None]
    part_max = jnp.max(jnp.where(member, top_p[:, :, None], NEG_FILL), axis=(0, 1))
    own_rows = device_place * local_rows + jnp.arange(local_rows, dtype=jnp.int32)
    part_norm = jnp.sum(
        jnp.where(own_rows[:, None] == seq_ends[None, :] - 1, state_norm[:, None], 0.0), axis=0
    )
    earlier_same = (owner_map[None, :] == owner_map[:, None]) & (
        seq_ids[None, :] < seq_ids[:, None]
    )
    slot_rank = jnp.sum(earlier_same.astype(jnp.int32), axis=1)
    device_ids = jnp.arange(plane_count * chip_count, dtype=jnp.int32)
    slot_hot = (owner_map[:, None, None] == device_ids[None, :, None]) & (
        slot_rank[:, None, None] == jnp.arange(SLOTS, dtype=jnp.int32)[None, None, :]
    )
    req_max = jnp.max(jnp.where(slot_hot, part_max[:, None, None], NEG_FILL), axis=0)
    req_norm = jnp.sum(jnp.where(slot_hot, part_norm[:, None, None], 0.0), axis=0)
    req = jnp.stack([req_max, req_norm], axis=2).reshape(plane_count, chip_count * SLOTS * 2)
    stats = jnp.stack([top_p, total_p, moment_p, chosen_p], axis=2).reshape(
        plane_count, local_rows * 4
    )
    outgoing = jnp.concatenate([stats, req], axis=1)
    incoming = lax.all_to_all(outgoing, PLANE, 0, 0, tiled=True)
    in_stats = incoming[:, : local_rows * 4].reshape(plane_count, local_rows, 4)
    tops = in_stats[:, :, 0]
    row_top = jnp.max(tops, axis=0)
    scale = jnp.exp(tops - row_top[None, :])
    row_total = jnp.sum(in_stats[:, :, 1] * scale, axis=0)
    row_moment = jnp.sum(in_stats[:, :, 2] * scale, axis=0)
    row_chosen = jnp.sum(in_stats[:, :, 3], axis=0)
    log_total = jnp.log(row_total)
    logprob = jnp.where(live_row, row_chosen - row_top - log_total, 0.0)
    entropy = jnp.where(live_row, row_top + log_total - row_moment / row_total, 0.0)
    in_req = incoming[:, local_rows * 4 :].reshape(plane_count, chip_count, SLOTS, 2)
    chip_max = jnp.max(in_req[..., 0], axis=0)
    chip_norm = jnp.sum(in_req[..., 1], axis=0)
    chip_pair = jnp.stack([chip_max, chip_norm], axis=2)
    got = lax.all_to_all(chip_pair, CHIP, 0, 0, tiled=True)
    final_max = jnp.max(got[..., 0], axis=0)
    final_norm = jnp.sum(got[..., 1], axis=0)
    has_slot = jnp.any(slot_hot[:, device_place, :], axis=0)
    request_table = jnp.where(has_slot[:, None], jnp.stack([final_max, final_norm], axis=1), 0.0)
    return (logprob, entropy, request_table[None])


def solution(mesh):
    tok_count, rep_count = mesh.devices.shape
    cores = 2
    side = int(round((tok_count // cores) ** 0.5))
    fine = Mesh(
        np.asarray(mesh.devices).reshape(side, tok_count // cores // side, cores, rep_count), AXES
    )
    tokens = P(AXES)
    return jax.shard_map(
        shards,
        mesh=fine,
        in_specs=(P(AXES, None), P(), P(("z", "y", "c"), None), tokens, P(), tokens, P()),
        out_specs=(tokens, tokens, P(AXES, None, None)),
        check_vma=False,
    )
```

profile of v0, /device:TPU:1, one launch (start us, length us, event | category | flops | bytes accessed | tf_op | source)
XLA Modules:
  0.0 252.8 jit_solution(15617818416284887751)
XLA Ops:
  7.2 0.7 fusion.13
  7.9 0.7 fusion.12
  8.6 0.7 constant_dynamic-update-slice_fusion
  9.4 0.7 convert_element_type.37
  10.1 0.9 fusion.6
  11.0 0.9 fusion.8
  11.9 0.1 copy.38
  12.0 2.1 dynamic_update_slice.8
  14.1 0.7 copy-done.1
  15.0 79.2 %all-reduce.5.cloned.1.call-done = bf16[1,8,25,1024]{3,1,0,2:T(8,128)(2,1)} async-done(((bf16[1,8,25,1024]{3,1,0,2:T(8,128)(2,1)}), bf16[1,8,25,1024]{3,1,0,2:T(8,128)(2,1)}) %all-reduce.5.cloned.1.call-update) | async-done | bytes 409616 | tf_op jit(solution)/shard_map/psum | solution.py:33
  94.2 0.4 broadcast_in_dim.109
  94.6 0.6 copy-done.2
  95.2 1.7 copy-done
  97.0 7.4 %collective-permute-start = (bf16[251,1024]{1,0:T(8,128)(2,1)}, bf16[251,1024]{1,0:T(8,128)(2,1)}, u32[]{:S(2)}, u32[]{:S(2)}) collective-permute-start(bf16[251,1024]{1,0:T(8,128)(2,1)} %param.15), channel_id=1, source_target_pairs={{0,4},{4,0},{1,5},{5,1},{2,6},{6,2},{3,7},{7,3},{8,12},{12,8},{9,1... | collective-permute-start | bytes 1542152 | tf_op jit(solution)/shard_map/ppermute | solution.py:53
  104.4 0.1 copy.40
  104.5 0.1 reduce-window.7
  104.6 0.1 reduce.13
  104.8 0.2 convert_reduce_fusion.1
  105.0 0.1 select_reduce_fusion.4
  105.2 1.4 convert_reduce_fusion
  106.6 0.1 iota_compare_fusion.1
  106.7 93.2 %all-reduce.7.cloned.1.call-done = bf16[64,25,1024]{2,0,1:T(8,128)(2,1)} async-done(((bf16[64,25,1024]{2,0,1:T(8,128)(2,1)}), bf16[64,25,1024]{2,0,1:T(8,128)(2,1)}) %all-reduce.7.cloned.1.call-update) | async-done | bytes 3276816 | tf_op jit(solution)/shard_map/psum | solution.py:33
  199.9 0.9 fusion.5
  200.8 0.1 slice_compare_fusion
  201.0 4.2 %fusion.16 = (f32[64,25]{0,1:T(8,128)S(1)}, f32[64,25,502]{2,0,1:T(8,128)S(1)}) fusion(bf16[64,25,1024]{2,0,1:T(8,128)(2,1)} %all-reduce.7.cloned.1.call-done, bf16[251,1024]{1,0:T(8,128)(2,1)} %collective-permute-done, bf16[251,1024]{1,0:T(8,128)(2,1)} %param.15), kind=kOutput, calls=%fused_computation.71 | convolution fusion | flops 1647811328 | bytes 7524096 | tf_op jit(solution)/shard_map/dot_general | solution.py:17
  205.2 0.1 copy.41
  205.3 0.9 select_reduce_fusion.1
  206.2 0.1 select_reduce_fusion.3
  206.3 1.0 copy.42
  207.4 1.7 reshape.263
  209.3 1.9 fusion
  211.3 0.7 copy.44
  211.9 9.8 %all-to-all-start = ((f32[64,1,128]{2,1,0:T(1,128)}), f32[64,1,128]{2,1,0:T(1,128)S(1)}, u32[]{:S(2)}, u32[]{:S(2)}) async-start(f32[64,1,128]{2,1,0:T(1,128)} %copy.44), calls=%async_computation | async-start | bytes 65536 | tf_op jit(solution)/shard_map/all_to_all | solution.py:106
  221.8 0.1 broadcast_and_fusion
  221.9 0.2 dynamic-slice_reduce_fusion
  222.1 10.5 %all-to-all-done = f32[64,1,128]{2,1,0:T(1,128)S(1)} async-done(((f32[64,1,128]{2,1,0:T(1,128)}), f32[64,1,128]{2,1,0:T(1,128)S(1)}, u32[]{:S(2)}, u32[]{:S(2)}) %all-to-all-start) | async-done | bytes 32800 | tf_op jit(solution)/shard_map/all_to_all | solution.py:106
  232.6 0.1 copy.45
  232.7 0.3 fusion.15
  233.0 0.1 slice_reduce_fusion.2
  233.1 0.1 copy.49
  233.2 0.1 copy.48
  233.3 0.7 copy.50
  234.0 6.4 %all-to-all-start.1 = ((f32[8,2,2]{1,2,0:T(2,128)}), f32[8,2,2]{1,2,0:T(2,128)S(1)}, u32[]{:S(2)}, u32[]{:S(2)}) async-start(f32[8,2,2]{1,2,0:T(2,128)} %copy.50), calls=%async_computation.1 | async-start | bytes 16384 | tf_op jit(solution)/shard_map/all_to_all | solution.py:121
  240.4 0.1 reduce_max.57
  240.5 0.2 multiply_reduce_fusion.1
  240.7 0.5 subtract_select_fusion
  241.2 4.0 %all-to-all-done.1 = f32[8,2,2]{1,2,0:T(2,128)S(1)} async-done(((f32[8,2,2]{1,2,0:T(2,128)}), f32[8,2,2]{1,2,0:T(2,128)S(1)}, u32[]{:S(2)}, u32[]{:S(2)}) %all-to-all-start.1) | async-done | bytes 160 | tf_op jit(solution)/shard_map/all_to_all | solution.py:121
  245.3 0.7 copy.51
  (44 shorter events, 0.8 us)
Async XLA Ops:
  7.2 87.0 %all-reduce.5.cloned.1.call-start = ((), (), s32[]{:S(2)}) async-start(), calls=%async_computation.2 | async-start | bytes 819200 | tf_op jit(solution)/shard_map/psum | solution.py:33
  14.1 0.8 copy-start.1
  14.9 185.0 %all-reduce.7.cloned.1.call-start = ((), (), s32[]{:S(2)}) async-start(), calls=%async_computation.3 | async-start | bytes 6553600 | tf_op jit(solution)/shard_map/psum | solution.py:33
  15.0 89.4 %copy-start.3 = (s32[64]{0:T(128)S(1)}, s32[64]{0:T(128)}, u32[]{:S(2)}) copy-start(s32[64]{0:T(128)} %param.17) | copy-start | bytes 772
  15.0 89.9 %copy-start.4 = (s32[64]{0:T(128)S(1)}, s32[64]{0:T(128)}, u32[]{:S(2)}) copy-start(s32[64]{0:T(128)} %param.19) | copy-start | bytes 772
  94.2 1.0 copy-start.2
  95.2 1.7 copy-start
  97.0 104.0 %collective-permute-start = (bf16[251,1024]{1,0:T(8,128)(2,1)}, bf16[251,1024]{1,0:T(8,128)(2,1)}, u32[]{:S(2)}, u32[]{:S(2)}) collective-permute-start(bf16[251,1024]{1,0:T(8,128)(2,1)} %param.15), channel_id=1, source_target_pairs={{0,4},{4,0},{1,5},{5,1},{2,6},{6,2},{3,7},{7,3},{8,12},{12,8},{9,1... | collective-permute-start | bytes 1542152 | tf_op jit(solution)/shard_map/ppermute | solution.py:53
  205.2 35.5 %copy-start.5 = (s32[24]{0:T(128)S(1)}, s32[24]{0:T(128)}, u32[]{:S(2)}) copy-start(s32[24]{0:T(128)} %param.18) | copy-start | bytes 292
  211.9 20.7 %all-to-all-start = ((f32[64,1,128]{2,1,0:T(1,128)}), f32[64,1,128]{2,1,0:T(1,128)S(1)}, u32[]{:S(2)}, u32[]{:S(2)}) async-start(f32[64,1,128]{2,1,0:T(1,128)} %copy.44), calls=%async_computation | async-start | bytes 65536 | tf_op jit(solution)/shard_map/all_to_all | solution.py:106
  234.0 11.3 %all-to-all-start.1 = ((f32[8,2,2]{1,2,0:T(2,128)}), f32[8,2,2]{1,2,0:T(2,128)S(1)}, u32[]{:S(2)}, u32[]{:S(2)}) async-start(f32[8,2,2]{1,2,0:T(2,128)} %copy.50), calls=%async_computation.1 | async-start | bytes 16384 | tf_op jit(solution)/shard_map/all_to_all | solution.py:121
Sparse Core Ops, SparseCore 0:
  15.0 79.1 all-reduce.4
  97.1 102.7 all-reduce.6
where the time goes:
time: 253 us
  waiting for transfers between devices  187 us (74%)
  starting transfers between devices  23.7 us (9%)
  between operations  14.4 us (6%)
  other arithmetic  12.4 us (5%)
  local copies, waits for them, and re-layouts  11.1 us (4%)
  matrix products  4.21 us (2%)
    psum x2, waiting for transfers between devices, gather_by_sum(): return lax.psum(buffer, axis)  172 us
    all_to_all x1, waiting for transfers between devices, shards(): incoming = lax.all_to_all(outgoing, PLANE, 0, 0, tiled=True)  10.5 us
    all_to_all x1, starting transfers between devices, shards(): incoming = lax.all_to_all(outgoing, PLANE, 0, 0, tiled=True)  9.85 us
    ppermute x1, starting transfers between devices, shards(): lax.ppermute(head_weight, 'c', [(i, (i + 1) % nc) for i in range(nc)])  7.37 us
    all_to_all x1, starting transfers between devices, shards(): got = lax.all_to_all(chip_pair, CHIP, 0, 0, tiled=True)  6.39 us
  transfers between devices with their start and end apart: 5, of which 4 were waited for; matrix products, arithmetic and copies ran while one was open for 2% of the time, Pallas kernels for 0%

commit v1 on v0

--- a/solution.py
+++ b/solution.py
@@ -30,7 +30,7 @@
     place = lax.axis_index(axis)
     buffer = jnp.zeros((count,) + block.shape, block.dtype)
     buffer = lax.dynamic_update_slice(buffer, block[None], (place,) + (0,) * block.ndim)
-    return lax.psum(buffer, axis)
+    return jnp.sum(lax.all_gather(buffer, axis), axis=0)
 
 
 def shards(hidden, norm_gain, head_weight, targets, lengths, padding_mask, owner_map):

time: 253 us -> 400 us (1.58)
  waiting for transfers between devices: 187 us -> 325 us
  other arithmetic: 12.4 us -> 27.8 us
  starting transfers between devices: 23.7 us -> 18.9 us
    all_gather x0 -> x2, waiting for transfers between devices: none -> 311 us  [gather_by_sum(): return jnp.sum(lax.all_gather(buffer, axis), axis=0)]
    psum x2 -> x0, waiting for transfers between devices: 172 us -> none  [gather_by_sum(): return lax.psum(buffer, axis)]
    reduce_sum x0 -> x2, other arithmetic: none -> 13.5 us  [gather_by_sum(): return jnp.sum(lax.all_gather(buffer, axis), axis=0)]
    ppermute x1, starting transfers between devices: 7.37 us -> 2.64 us  [shards(): lax.ppermute(head_weight, 'c', [(i, (i + 1) % nc) for i in range(nc)])]
  transfers between devices with their start and end apart: 5 -> 5, of which waited for: 4 -> 4; matrix products, arithmetic and copies ran while one was open for 2% -> 4% of each run, Pallas kernels for 0% -> 0%
where the time goes in v1:
time: 400 us
  waiting for transfers between devices  325 us (81%)
  other arithmetic  27.8 us (7%)
  starting transfers between devices  18.9 us (5%)
  between operations  14.4 us (4%)
  local copies, waits for them, and re-layouts  10.4 us (3%)
    all_gather x2, waiting for transfers between devices, gather_by_sum(): return jnp.sum(lax.all_gather(buffer, axis), axis=0)  311 us
    reduce_sum x2, other arithmetic, gather_by_sum(): return jnp.sum(lax.all_gather(buffer, axis), axis=0)  13.5 us
    all_to_all x1, waiting for transfers between devices, shards(): incoming = lax.all_to_all(outgoing, PLANE, 0, 0, tiled=True)  10.5 us
    all_to_all x1, starting transfers between devices, shards(): incoming = lax.all_to_all(outgoing, PLANE, 0, 0, tiled=True)  9.8 us
  transfers between devices with their start and end apart: 5, of which 4 were waited for; matrix products, arithmetic and copies ran while one was open for 4% of the time, Pallas kernels for 0%

profile of v1, /device:TPU:1, one launch (start us, length us, event | category | flops | bytes accessed | tf_op | source)
XLA Modules:
  0.0 399.9 jit_solution(13910792004376625661)
XLA Ops:
  7.2 0.9 fusion.6
  8.1 0.7 convert_element_type.41
  8.8 0.7 fusion.13
  9.5 0.7 fusion.12
  10.2 0.7 constant_dynamic-update-slice_fusion
  11.0 0.9 fusion.8
  12.0 2.1 dynamic_update_slice.8
  14.1 0.7 copy-done.1
  15.0 54.1 %all-gather.3.cloned.1.call-done = bf16[8,8,25,1024]{3,1,2,0:T(8,128)(2,1)} async-done(((bf16[1,8,25,1024]{3,1,2,0:T(8,128)(2,1)}), bf16[8,8,25,1024]{3,1,2,0:T(8,128)(2,1)}) %all-gather.3.cloned.1.call-update) | async-done | bytes 3276816 | tf_op jit(solution)/shard_map/all_gather | solution.py:33
  69.0 3.4 reduce_sum.142
  72.5 0.4 broadcast_in_dim.65
  72.9 0.6 copy-done.2
  73.5 1.7 copy-done
  75.2 2.6 collective-permute-start
  77.9 0.1 copy.78
  78.0 0.1 reduce-window.7
  78.1 0.1 reduce.15
  78.3 0.2 convert_reduce_fusion.1
  78.5 0.6 select_reduce_fusion.4
  79.2 2.0 convert_reduce_fusion
  81.2 0.5 iota_compare_fusion.3
  81.7 0.7 iota_compare_fusion.1
  82.4 256.7 %all-gather.5.cloned.1.call-done = bf16[8,8,8,25,1024]{4,2,3,1,0:T(8,128)(2,1)} async-done(((bf16[1,8,8,25,1024]{4,2,3,1,0:T(8,128)(2,1)}), bf16[8,8,8,25,1024]{4,2,3,1,0:T(8,128)(2,1)}) %all-gather.5.cloned.1.call-update) | async-done | bytes 26214416 | tf_op jit(solution)/shard_map/all_gather | solution.py:33
  339.1 10.0 %reduce_sum.143 = bf16[8,8,25,1024]{3,1,2,0:T(8,128)(2,1)S(1)} reduce(bf16[8,8,8,25,1024]{4,2,3,1,0:T(8,128)(2,1)} %all-gather.5.cloned.1.call-done, bf16[]{:T(256)} %constant.149.clone.1), dimensions={0}, to_apply=%region_2.3 | reduce | flops 11468800 | bytes 29491202 | tf_op jit(solution)/shard_map/reduce_sum | solution.py:33
  349.2 0.4 copy.97
  349.6 0.7 fusion.9
  350.3 0.8 copy.92
  351.2 3.2 fusion.16
  354.5 1.9 fusion
  356.5 0.9 select_reduce_fusion.1
  357.4 0.1 select_reduce_fusion.3
  357.6 0.3 copy.80
  357.8 0.7 reshape.269
  358.7 0.7 copy.82
  359.4 9.8 %all-to-all-start = ((f32[64,1,128]{2,1,0:T(1,128)}), f32[64,1,128]{2,1,0:T(1,128)S(1)}, u32[]{:S(2)}, u32[]{:S(2)}) async-start(f32[64,1,128]{2,1,0:T(1,128)} %copy.82), calls=%async_computation | async-start | bytes 65536 | tf_op jit(solution)/shard_map/all_to_all | solution.py:106
  369.2 0.1 broadcast_and_fusion
  369.3 0.2 dynamic-slice_reduce_fusion
  369.5 10.5 %all-to-all-done = f32[64,1,128]{2,1,0:T(1,128)S(1)} async-done(((f32[64,1,128]{2,1,0:T(1,128)}), f32[64,1,128]{2,1,0:T(1,128)S(1)}, u32[]{:S(2)}, u32[]{:S(2)}) %all-to-all-start) | async-done | bytes 32800 | tf_op jit(solution)/shard_map/all_to_all | solution.py:106
  380.0 0.1 copy.83
  380.1 0.1 slice_reduce_fusion.2
  380.4 0.7 copy.88
  381.1 6.4 %all-to-all-start.1 = ((f32[8,2,2]{1,2,0:T(2,128)}), f32[8,2,2]{1,2,0:T(2,128)S(1)}, u32[]{:S(2)}, u32[]{:S(2)}) async-start(f32[8,2,2]{1,2,0:T(2,128)} %copy.88), calls=%async_computation.1 | async-start | bytes 16384 | tf_op jit(solution)/shard_map/all_to_all | solution.py:121
  387.5 0.3 fusion.15
  387.8 0.1 reduce_max.57
  387.9 0.2 multiply_reduce_fusion.1
  388.1 0.5 subtract_select_fusion
  388.6 3.8 all-to-all-done.1
  392.4 0.7 copy.89
  (55 shorter events, 1.1 us)
Async XLA Ops:
  7.2 61.9 %all-gather.3.cloned.1.call-start = ((), (), s32[]{:S(2)}) async-start(), calls=%async_computation.2 | async-start | bytes 3686400 | tf_op jit(solution)/shard_map/all_gather | solution.py:33
  14.1 0.8 copy-start.1
  14.9 324.2 %all-gather.5.cloned.1.call-start = ((), (), s32[]{:S(2)}) async-start(), calls=%async_computation.3 | async-start | bytes 29491200 | tf_op jit(solution)/shard_map/all_gather | solution.py:33
  72.5 1.0 copy-start.2
  72.5 5.4 %copy-start.7 = (s32[64]{0:T(128)S(1)}, s32[64]{0:T(128)}, u32[]{:S(2)}) copy-start(s32[64]{0:T(128)} %param.17) | copy-start | bytes 772
  72.5 5.9 %copy-start.8 = (s32[64]{0:T(128)S(1)}, s32[64]{0:T(128)}, u32[]{:S(2)}) copy-start(s32[64]{0:T(128)} %param.19) | copy-start | bytes 772
  73.5 1.7 copy-start
  75.2 276.0 %collective-permute-start = (bf16[251,1024]{1,0:T(8,128)(2,1)}, bf16[251,1024]{1,0:T(8,128)(2,1)}, u32[]{:S(2)}, u32[]{:S(2)}) collective-permute-start(bf16[251,1024]{1,0:T(8,128)(2,1)} %param.15), channel_id=1, source_target_pairs={{0,4},{4,0},{1,5},{5,1},{2,6},{6,2},{3,7},{7,3},{8,12},{12,8},{9,1... | collective-permute-start | bytes 1542152 | tf_op jit(solution)/shard_map/ppermute | solution.py:53
  354.4 2.1 copy-start.4
  354.4 2.9 copy-start.3
  354.4 2.9 copy-start.5
  354.4 2.9 copy-start.6
  354.5 33.6 %copy-start.9 = (s32[24]{0:T(128)S(1)}, s32[24]{0:T(128)}, u32[]{:S(2)}) copy-start(s32[24]{0:T(128)} %param.18) | copy-start | bytes 292
  359.4 20.6 %all-to-all-start = ((f32[64,1,128]{2,1,0:T(1,128)}), f32[64,1,128]{2,1,0:T(1,128)S(1)}, u32[]{:S(2)}, u32[]{:S(2)}) async-start(f32[64,1,128]{2,1,0:T(1,128)} %copy.82), calls=%async_computation | async-start | bytes 65536 | tf_op jit(solution)/shard_map/all_to_all | solution.py:106
  381.1 11.3 %all-to-all-start.1 = ((f32[8,2,2]{1,2,0:T(2,128)}), f32[8,2,2]{1,2,0:T(2,128)S(1)}, u32[]{:S(2)}, u32[]{:S(2)}) async-start(f32[8,2,2]{1,2,0:T(2,128)} %copy.88), calls=%async_computation.1 | async-start | bytes 16384 | tf_op jit(solution)/shard_map/all_to_all | solution.py:121
Sparse Core Ops, SparseCore 0:
  15.0 53.9 all-gather.2
  75.3 263.7 all-gather.4
